TPU v7x, 256 devices: a whole 4x4x8 slice. The times are simulated.
256 devices in a mesh: dp: 32 (over y, z_hi, core), tensor: 8 (over z_lo, x).
Axes of the slice: x: 4, y: 4, z: 8 (z_hi: 4, z_lo: 2; z = z_hi * 2 + z_lo), core: 2. Of those that a mesh axis runs over, the one named last changes fastest.
Arguments:
- inputs: bfloat16 [32768, 2048], P(('dp', 'tensor')), may hold values from -6 to 6
- norm_gain: float32 [2048], replicated, may hold values from 0.1 to 1.9
- proj_weight: bfloat16 [2048, 3, 2048], P('dp', None, 'tensor'), may hold values from -0.125 to 0.125
- filters: float32 [3, 7, 2048], P(None, None, 'tensor'), may hold values from -2.4 to 2.4
- cotangent: bfloat16 [32768, 2048], P('dp', 'tensor'), may hold values from -18 to 18
Outputs:
- mixed: bfloat16 [32768, 2048], P('dp', 'tensor')
- grad_inputs: bfloat16 [32768, 2048], P(('dp', 'tensor'))
- grad_proj: bfloat16 [2048, 3, 2048], P('dp', None, 'tensor')
- grad_filters: float32 [3, 7, 2048], P(None, None, 'tensor')
- grad_gain: float32 [2048], replicated
All inputs are finite; a program needn't handle non-finite values.
Results may differ from a plain program's by a relative error of at most 0.02.
Values may be sent and summed in bfloat16 or wider, within the bound.
No kernel may reach another device: no remote copies, remote signals or barrier semaphores. Data moves between devices by JAX's collectives and lax.ppermute only.
A program may use at most 64 MiB of HBM per device.

v0:
```python
import jax
import jax.numpy as jnp
from jax import lax
from jax.sharding import PartitionSpec as P


def passed_along(shard, axis, by):
    size = lax.axis_size(axis)
    pairs = [(i, i + by) for i in range(size) if 0 <= i + by < size]
    return lax.ppermute(shard, axis, pairs)


def body(inputs, norm_gain, proj_weight, filters, cotangent):
    taps = filters.shape[1]
    width = taps - 1
    wide = inputs.astype(jnp.float32)
    inv_rms = lax.rsqrt(jnp.mean(wide * wide, axis=1, keepdims=True) + 1e-05)
    normed = (wide * inv_rms * norm_gain).astype(jnp.bfloat16)
    weights = lax.all_gather(proj_weight, "dp", axis=0, tiled=True)
    positions = lax.all_gather(normed, "tensor", axis=0, tiled=True)
    length = positions.shape[0]
    streams = jnp.einsum(
        "td,dsc->tsc", positions, weights, preferred_element_type=jnp.float32
    ).astype(jnp.bfloat16)
    before = passed_along(streams[length - width :], "dp", 1)
    extended = jnp.concatenate([before, streams], axis=0).astype(jnp.float32)
    conv = jnp.zeros(streams.shape, jnp.float32)
    for tap in range(taps):
        conv = conv + filters[:, tap, :] * extended[width - tap : width - tap + length]
    mixed = (conv[:, 0] * conv[:, 1] * conv[:, 2]).astype(jnp.bfloat16)
    grad_out = cotangent.astype(jnp.float32)
    grad_conv = jnp.stack(
        [
            grad_out * conv[:, 1] * conv[:, 2],
            grad_out * conv[:, 0] * conv[:, 2],
            grad_out * conv[:, 0] * conv[:, 1],
        ],
        axis=1,
    )
    after = passed_along(grad_conv[:width], "dp", -1)
    grad_extended = jnp.concatenate([grad_conv, after], axis=0)
    grad_acc = jnp.zeros(streams.shape, jnp.float32)
    for tap in range(taps):
        grad_acc = grad_acc + filters[:, tap, :] * grad_extended[tap : tap + length]
    grad_streams = grad_acc.astype(jnp.bfloat16)
    filter_local = jnp.stack(
        [
            jnp.sum(grad_conv * extended[width - tap : width - tap + length], axis=0)
            for tap in range(taps)
        ],
        axis=1,
    )
    normed_terms = jnp.einsum(
        "tsc,dsc->td", grad_streams, weights, preferred_element_type=jnp.float32
    )
    grad_normed = lax.psum_scatter(
        normed_terms.astype(jnp.bfloat16), "tensor", scatter_dimension=0, tiled=True
    ).astype(jnp.float32)
    weight_terms = jnp.einsum(
        "td,tsc->dsc", positions, grad_streams, preferred_element_type=jnp.float32
    )
    grad_proj = lax.psum_scatter(
        weight_terms.astype(jnp.bfloat16), "dp", scatter_dimension=0, tiled=True
    )
    scaled = norm_gain * grad_normed
    grad_inputs = inv_rms * (
        scaled - wide * inv_rms * inv_rms * jnp.mean(scaled * wide, axis=1, keepdims=True)
    )
    gain_local = jnp.sum(grad_normed * wide * inv_rms, axis=0)
    grad_filters = lax.psum(filter_local, "dp")
    grad_gain = lax.psum(gain_local, ("dp", "tensor"))
    return (mixed, grad_inputs.astype(jnp.bfloat16), grad_proj, grad_filters, grad_gain)


def solution(mesh):
    return jax.shard_map(
        body,
        mesh=mesh,
        in_specs=(
            P(("dp", "tensor"), None),
            P(),
            P("dp", None, "tensor"),
            P(None, None, "tensor"),
            P("dp", "tensor"),
        ),
        out_specs=(
            P("dp", "tensor"),
            P(("dp", "tensor"), None),
            P("dp", None, "tensor"),
            P(None, None, "tensor"),
            P(),
        ),
        check_vma=False,
    )
```

profile of v0, /device:TPU:1, one launch (start us, length us, event | category | flops | bytes accessed | tf_op | source)
XLA Modules:
  0.0 393.9 jit_solution(4973453960555978686)
XLA Ops:
  7.2 0.7 all-gather.5.cloned.1.call-update
  7.9 1.2 fusion.26
  9.2 2.0 fusion.20
  11.3 1.0 fusion.30
  12.3 59.7 %all-gather.5.cloned.1.call-done = bf16[2048,3,256]{2,0,1:T(8,128)(2,1)} async-done(((bf16[64,3,256]{2,0,1:T(8,128)(2,1)}), bf16[2048,3,256]{2,0,1:T(8,128)(2,1)}) %all-gather.5.cloned.1.call-update) | async-done | bytes 3145744 | tf_op jit(solution)/shard_map/all_gather | solution.py:19
  72.0 54.9 %all-gather.3.cloned.1.call-done = bf16[1024,2048]{1,0:T(8,128)(2,1)} async-done(((bf16[128,2048]{1,0:T(8,128)(2,1)}), bf16[1024,2048]{1,0:T(8,128)(2,1)}) %all-gather.3.cloned.1.call-update) | async-done | bytes 4194320 | tf_op jit(solution)/shard_map/all_gather | solution.py:20
  126.9 6.6 %fusion.14 = bf16[1024,3,256]{2,0,1:T(8,128)(2,1)S(1)} fusion(bf16[2048,3,256]{2,0,1:T(8,128)(2,1)} %all-gather.5.cloned.1.call-done, bf16[1024,2048]{1,0:T(8,128)(2,1)} %all-gather.3.cloned.1.call-done), kind=kOutput, calls=%fused_computation.33 | convolution fusion | flops 3222011904 | bytes 8912896 | tf_op jit(solution)/shard_map/td,dsc->tsc/dot_general | solution.py:22
  133.5 4.7 %collective-permute-start = (bf16[6,3,256]{2,0,1:T(8,128)(2,1)S(1)}, bf16[6,3,256]{2,0,1:T(8,128)(2,1)S(1)}, u32[]{:S(2)}, u32[]{:S(2)}) collective-permute-start(bf16[6,3,256]{2,0,1:T(8,128)(2,1)S(1)} %slice.120), channel_id=1, source_target_pairs={{0,8},{8,16},{16,24},{24,32},{32,40},{40,48},{48,56},{56,64},{64,7... | collective-permute-start | bytes 27656 | tf_op jit(solution)/shard_map/ppermute | solution.py:10
  138.3 0.8 collective-permute-done
  139.1 0.3 maximum_convert_fusion
  139.4 2.6 multiply_add_fusion
  142.0 1.2 fusion.25
  143.2 2.9 multiply_reduce_fusion
  146.0 1.9 collective-permute-start.1
  148.0 4.8 %collective-permute-done.1 = f32[6,3,256]{2,0,1:T(8,128)S(1)} collective-permute-done((f32[6,3,256]{2,0,1:T(8,128)S(1)}, f32[6,3,256]{2,0,1:T(8,128)S(1)}, u32[]{:S(2)}, u32[]{:S(2)}) %collective-permute-start.1) | collective-permute-done | bytes 18464 | tf_op jit(solution)/shard_map/ppermute | solution.py:10
  153.0 2.7 fusion.8
  155.8 5.1 %bitcast_convert_fusion = bf16[1024,2048]{1,0:T(8,128)(2,1)} fusion(bf16[1024,3,256]{2,0,1:T(8,128)(2,1)S(1)} %fusion.8, bf16[2048,3,256]{2,0,1:T(8,128)(2,1)S(1)} %copy-done.3), kind=kOutput, calls=%fused_computation | convolution fusion | flops 3223322624 | bytes 8912896 | tf_op jit(solution)/shard_map/tsc,dsc->td/dot_general | solution.py:53
  160.9 0.2 reduce-scatter.5.cloned.1.call-start
  161.1 7.5 %fusion.4 = bf16[2048,3,256]{2,0,1:T(8,128)(2,1)} fusion(bf16[1024,3,256]{2,0,1:T(8,128)(2,1)S(1)} %fusion.8, bf16[1024,2048]{1,0:T(8,128)(2,1)} %all-gather.3.cloned.1.call-done), kind=kOutput, calls=%fused_computation.5 | convolution fusion | flops 3222798336 | bytes 8912896 | tf_op jit(solution)/shard_map/td,tsc->dsc/dot_general | solution.py:59
  168.7 135.1 %psum.14 = f32[3,7,256]{2,0,1:T(4,128)S(1)} all-reduce(f32[3,7,256]{2,0,1:T(4,128)S(1)} %constant_dynamic-update-slice_fusion), channel_id=1, replica_groups=mesh['dp'=32,'tensor'=8] {'dp'}, use_global_device_ids=true, to_apply=%region_11.0 | all-reduce | flops 5376 | bytes 43008 | tf_op jit(solution)/shard_map/psum | solution.py:70
  303.8 0.6 copy.12
  304.5 1.4 fusion.29
  305.8 79.3 %psum.15 = f32[2048]{0:T(1024)} all-reduce(f32[2048]{0:T(1024)S(1)} %get-tuple-element.17), channel_id=1, replica_groups=mesh['dp'=32,'tensor'=8] {'dp','tensor'}, use_global_device_ids=true, to_apply=%region_13.0 | all-reduce | flops 2048 | bytes 16384 | tf_op jit(solution)/shard_map/psum | solution.py:71
  385.2 2.2 fusion.23
  (32 shorter events, 0.5 us)
Async XLA Ops:
  7.2 64.9 %all-gather.5.cloned.1.call-start = ((), (), s32[]{:S(2)}) async-start(), calls=%async_computation.3 | async-start | bytes 3244032 | tf_op jit(solution)/shard_map/all_gather | solution.py:19
  7.9 119.0 %all-gather.3.cloned.1.call-start = ((), (), s32[]{:S(2)}) async-start(), calls=%async_computation.2 | async-start | bytes 4718592 | tf_op jit(solution)/shard_map/all_gather | solution.py:20
  11.2 293.2 %reduce-scatter.3.cloned.1.call-start = ((), (), s32[]{:S(2)}) async-start(), calls=%async_computation.4 | async-start | bytes 4718592 | tf_op jit(solution)/shard_map/reduce_scatter | solution.py:56
  133.5 5.5 %collective-permute-start = (bf16[6,3,256]{2,0,1:T(8,128)(2,1)S(1)}, bf16[6,3,256]{2,0,1:T(8,128)(2,1)S(1)}, u32[]{:S(2)}, u32[]{:S(2)}) collective-permute-start(bf16[6,3,256]{2,0,1:T(8,128)(2,1)S(1)} %slice.120), channel_id=1, source_target_pairs={{0,8},{8,16},{16,24},{24,32},{32,40},{40,48},{48,56},{56,64},{64,7... | collective-permute-start | bytes 27656 | tf_op jit(solution)/shard_map/ppermute | solution.py:10
  139.4 2.6 copy-start.1
  146.0 6.8 %collective-permute-start.1 = (f32[6,3,256]{2,0,1:T(8,128)S(1)}, f32[6,3,256]{2,0,1:T(8,128)S(1)}, u32[]{:S(2)}, u32[]{:S(2)}) collective-permute-start(f32[6,3,256]{2,0,1:T(8,128)S(1)} %slice.131), channel_id=1, source_target_pairs={{8,0},{16,8},{24,16},{32,24},{40,32},{48,40},{56,48},{64,56},{72,6... | collective-permute-start | bytes 55304 | tf_op jit(solution)/shard_map/ppermute | solution.py:10
  153.0 2.7 copy-start.3
  160.9 226.5 %reduce-scatter.5.cloned.1.call-start = ((), (), s32[]{:S(2)}) async-start(), calls=%async_computation.5 | async-start | bytes 3244032 | tf_op jit(solution)/shard_map/reduce_scatter | solution.py:62
  168.6 135.8 %copy-start = (bf16[128,2048]{1,0:T(8,128)(2,1)S(1)}, bf16[128,2048]{1,0:T(8,128)(2,1)}, u32[]{:S(2)}) copy-start(bf16[128,2048]{1,0:T(8,128)(2,1)} %param.5) | copy-start | bytes 1572868
  168.6 135.8 %copy-start.2 = (f32[2048]{0:T(1024)S(1)}, f32[2048]{0:T(1024)}, u32[]{:S(2)}) copy-start(f32[2048]{0:T(1024)} %param.6) | copy-start | bytes 24580
Sparse Core Ops, SparseCore 0:
  10.7 61.3 all-gather.4
  74.4 52.5 all-gather.2
  161.0 54.1 reduce-scatter.2
  219.5 92.7 reduce-scatter.4
where the time goes:
time: 394 us
  blocking collectives  214 us (54%)
  waiting for transfers between devices  121 us (31%)
  matrix products  19.2 us (5%)
  other arithmetic  16.6 us (4%)
  between operations  13.9 us (4%)
  starting transfers between devices  6.99 us (2%)
    psum x1, blocking collectives, body(): grad_filters = lax.psum(filter_local, 'dp')  135 us
    psum x1, blocking collectives, body(): grad_gain = lax.psum(gain_local, ('dp', 'tensor'))  79.3 us
    all_gather x1, waiting for transfers between devices, body(): weights = lax.all_gather(proj_weight, 'dp', axis=0, tiled=True)  59.7 us
    all_gather x1, waiting for transfers between devices, body(): positions = lax.all_gather(normed, 'tensor', axis=0, tiled=True)  54.9 us
  transfers between devices with their start and end apart: 6, of which 4 were waited for; matrix products, arithmetic and copies ran while one was open for 4% of the time, Pallas kernels for 0%

commit v1 on v0

--- a/solution.py
+++ b/solution.py
@@ -68,7 +68,7 @@
     )
     gain_local = jnp.sum(grad_normed * wide * inv_rms, axis=0)
     grad_filters = lax.psum(filter_local, "dp")
-    grad_gain = lax.psum(gain_local, ("dp", "tensor"))
+    grad_gain = lax.psum(lax.psum(gain_local, "tensor"), "dp")
     return (mixed, grad_inputs.astype(jnp.bfloat16), grad_proj, grad_filters, grad_gain)
 
 

time: 394 us -> 382 us (0.970); the launches traced: 394 us -> 376 us
  blocking collectives: 214 us -> 151 us
  waiting for transfers between devices: 121 us -> 167 us
    psum x1, blocking collectives: 79.3 us -> 13.4 us  [body(): grad_gain = lax.psum(lax.psum(gain_local, 'tensor'), 'dp')]
    reduce_scatter x1, waiting for transfers between devices: 0.01 us -> 45.6 us  [body(): lax.psum_scatter(normed_terms.astype(jnp.bfloat16), 'tensor', scatter_dim...]
  transfers between devices with their start and end apart: 6 -> 6, of which waited for: 4 -> 5; matrix products, arithmetic and copies ran while one was open for 4% -> 4% of each run, Pallas kernels for 0% -> 0%
where the time goes in v1:
time: 382 us; the launch traced here: 376 us
  waiting for transfers between devices  167 us (44%)
  blocking collectives  151 us (40%)
  matrix products  19.2 us (5%)
  other arithmetic  16.6 us (4%)
  between operations  13.9 us (4%)
  starting transfers between devices  6.99 us (2%)
    psum x1, blocking collectives, body(): grad_filters = lax.psum(filter_local, 'dp')  138 us
    all_gather x1, waiting for transfers between devices, body(): weights = lax.all_gather(proj_weight, 'dp', axis=0, tiled=True)  59.7 us
    all_gather x1, waiting for transfers between devices, body(): positions = lax.all_gather(normed, 'tensor', axis=0, tiled=True)  54.9 us
    reduce_scatter x1, waiting for transfers between devices, body(): lax.psum_scatter(normed_terms.astype(jnp.bfloat16), 'tensor', scatter_dim...  45.6 us
    psum x1, blocking collectives, body(): grad_gain = lax.psum(lax.psum(gain_local, 'tensor'), 'dp')  13.4 us
  transfers between devices with their start and end apart: 6, of which 5 were waited for; matrix products, arithmetic and copies ran while one was open for 4% of the time, Pallas kernels for 0%

profile of v1, /device:TPU:1, one launch (start us, length us, event | category | flops | bytes accessed | tf_op | source)
XLA Modules:
  0.0 376.2 jit_solution(13106994097221643583)
XLA Ops:
  7.2 0.7 all-gather.5.cloned.1.call-update
  7.9 1.2 fusion.26
  9.2 2.0 fusion.20
  11.3 1.0 fusion.30
  12.3 59.7 %all-gather.5.cloned.1.call-done = bf16[2048,3,256]{2,0,1:T(8,128)(2,1)} async-done(((bf16[64,3,256]{2,0,1:T(8,128)(2,1)}), bf16[2048,3,256]{2,0,1:T(8,128)(2,1)}) %all-gather.5.cloned.1.call-update) | async-done | bytes 3145744 | tf_op jit(solution)/shard_map/all_gather | solution.py:19
  72.0 54.9 %all-gather.3.cloned.1.call-done = bf16[1024,2048]{1,0:T(8,128)(2,1)} async-done(((bf16[128,2048]{1,0:T(8,128)(2,1)}), bf16[1024,2048]{1,0:T(8,128)(2,1)}) %all-gather.3.cloned.1.call-update) | async-done | bytes 4194320 | tf_op jit(solution)/shard_map/all_gather | solution.py:20
  126.9 6.6 %fusion.14 = bf16[1024,3,256]{2,0,1:T(8,128)(2,1)S(1)} fusion(bf16[2048,3,256]{2,0,1:T(8,128)(2,1)} %all-gather.5.cloned.1.call-done, bf16[1024,2048]{1,0:T(8,128)(2,1)} %all-gather.3.cloned.1.call-done), kind=kOutput, calls=%fused_computation.33 | convolution fusion | flops 3222011904 | bytes 8912896 | tf_op jit(solution)/shard_map/td,dsc->tsc/dot_general | solution.py:22
  133.5 4.7 %collective-permute-start = (bf16[6,3,256]{2,0,1:T(8,128)(2,1)S(1)}, bf16[6,3,256]{2,0,1:T(8,128)(2,1)S(1)}, u32[]{:S(2)}, u32[]{:S(2)}) collective-permute-start(bf16[6,3,256]{2,0,1:T(8,128)(2,1)S(1)} %slice.120), channel_id=1, source_target_pairs={{0,8},{8,16},{16,24},{24,32},{32,40},{40,48},{48,56},{56,64},{64,7... | collective-permute-start | bytes 27656 | tf_op jit(solution)/shard_map/ppermute | solution.py:10
  138.3 0.8 collective-permute-done
  139.1 0.3 maximum_convert_fusion
  139.4 2.6 multiply_add_fusion
  142.0 1.2 fusion.25
  143.2 2.9 multiply_reduce_fusion
  146.0 1.9 collective-permute-start.1
  148.0 4.8 %collective-permute-done.1 = f32[6,3,256]{2,0,1:T(8,128)S(1)} collective-permute-done((f32[6,3,256]{2,0,1:T(8,128)S(1)}, f32[6,3,256]{2,0,1:T(8,128)S(1)}, u32[]{:S(2)}, u32[]{:S(2)}) %collective-permute-start.1) | collective-permute-done | bytes 18464 | tf_op jit(solution)/shard_map/ppermute | solution.py:10
  153.0 2.7 fusion.8
  155.8 5.1 %bitcast_convert_fusion = bf16[1024,2048]{1,0:T(8,128)(2,1)} fusion(bf16[1024,3,256]{2,0,1:T(8,128)(2,1)S(1)} %fusion.8, bf16[2048,3,256]{2,0,1:T(8,128)(2,1)S(1)} %copy-done.3), kind=kOutput, calls=%fused_computation | convolution fusion | flops 3223322624 | bytes 8912896 | tf_op jit(solution)/shard_map/tsc,dsc->td/dot_general | solution.py:53
  161.1 7.5 %fusion.4 = bf16[2048,3,256]{2,0,1:T(8,128)(2,1)} fusion(bf16[1024,3,256]{2,0,1:T(8,128)(2,1)S(1)} %fusion.8, bf16[1024,2048]{1,0:T(8,128)(2,1)} %all-gather.3.cloned.1.call-done), kind=kOutput, calls=%fused_computation.5 | convolution fusion | flops 3222798336 | bytes 8912896 | tf_op jit(solution)/shard_map/td,tsc->dsc/dot_general | solution.py:59
  168.7 45.6 %reduce-scatter.3.cloned.1.call-done = bf16[128,2048]{1,0:T(8,128)(2,1)} async-done(((bf16[1024,2048]{1,0:T(8,128)(2,1)}), bf16[128,2048]{1,0:T(8,128)(2,1)}) %reduce-scatter.3.cloned.1.call-update) | async-done | bytes 524304 | tf_op jit(solution)/shard_map/reduce_scatter | solution.py:56
  214.3 1.4 fusion.29
  215.7 13.4 %psum.22 = f32[2048]{0:T(1024)S(1)} all-reduce(f32[2048]{0:T(1024)S(1)} %get-tuple-element.17), channel_id=1, replica_groups=mesh['dp'=32,'tensor'=8] {'tensor'}, use_global_device_ids=true, to_apply=%region_13.0 | all-reduce | flops 2048 | bytes 16384 | tf_op jit(solution)/shard_map/psum | solution.py:71
  229.1 137.8 %all-reduce = (f32[3,7,256]{2,0,1:T(4,128)S(1)}, f32[2048]{0:T(1024)}) all-reduce(f32[3,7,256]{2,0,1:T(4,128)S(1)} %constant_dynamic-update-slice_fusion, f32[2048]{0:T(1024)S(1)} %psum.22), channel_id=1, replica_groups=mesh['dp'=32,'tensor'=8] {'dp'}, use_global_device_ids=true, to_apply=%region_11.0 | all-reduce | flops 7424 | bytes 59392 | tf_op jit(solution)/shard_map/psum | solution.py:70
  366.8 0.6 copy.12
  367.5 2.2 fusion.23
  (32 shorter events, 0.7 us)
Async XLA Ops:
  7.2 64.9 %all-gather.5.cloned.1.call-start = ((), (), s32[]{:S(2)}) async-start(), calls=%async_computation.3 | async-start | bytes 3244032 | tf_op jit(solution)/shard_map/all_gather | solution.py:19
  7.9 119.0 %all-gather.3.cloned.1.call-start = ((), (), s32[]{:S(2)}) async-start(), calls=%async_computation.2 | async-start | bytes 4718592 | tf_op jit(solution)/shard_map/all_gather | solution.py:20
  11.2 203.0 %reduce-scatter.3.cloned.1.call-start = ((), (), s32[]{:S(2)}) async-start(), calls=%async_computation.4 | async-start | bytes 4718592 | tf_op jit(solution)/shard_map/reduce_scatter | solution.py:56
  133.5 5.5 %collective-permute-start = (bf16[6,3,256]{2,0,1:T(8,128)(2,1)S(1)}, bf16[6,3,256]{2,0,1:T(8,128)(2,1)S(1)}, u32[]{:S(2)}, u32[]{:S(2)}) collective-permute-start(bf16[6,3,256]{2,0,1:T(8,128)(2,1)S(1)} %slice.120), channel_id=1, source_target_pairs={{0,8},{8,16},{16,24},{24,32},{32,40},{40,48},{48,56},{56,64},{64,7... | collective-permute-start | bytes 27656 | tf_op jit(solution)/shard_map/ppermute | solution.py:10
  139.4 2.6 copy-start.1
  146.0 6.8 %collective-permute-start.1 = (f32[6,3,256]{2,0,1:T(8,128)S(1)}, f32[6,3,256]{2,0,1:T(8,128)S(1)}, u32[]{:S(2)}, u32[]{:S(2)}) collective-permute-start(f32[6,3,256]{2,0,1:T(8,128)S(1)} %slice.131), channel_id=1, source_target_pairs={{8,0},{16,8},{24,16},{32,24},{40,32},{48,40},{56,48},{64,56},{72,6... | collective-permute-start | bytes 55304 | tf_op jit(solution)/shard_map/ppermute | solution.py:10
  153.0 2.7 copy-start.3
  160.9 208.8 %reduce-scatter.5.cloned.1.call-start = ((), (), s32[]{:S(2)}) async-start(), calls=%async_computation.5 | async-start | bytes 3244032 | tf_op jit(solution)/shard_map/reduce_scatter | solution.py:62
  168.6 45.7 %copy-start = (bf16[128,2048]{1,0:T(8,128)(2,1)S(1)}, bf16[128,2048]{1,0:T(8,128)(2,1)}, u32[]{:S(2)}) copy-start(bf16[128,2048]{1,0:T(8,128)(2,1)} %param.5) | copy-start | bytes 1572868
  168.6 45.7 %copy-start.2 = (f32[2048]{0:T(1024)S(1)}, f32[2048]{0:T(1024)}, u32[]{:S(2)}) copy-start(f32[2048]{0:T(1024)} %param.6) | copy-start | bytes 24580
Sparse Core Ops, SparseCore 0:
  10.7 61.3 all-gather.4
  74.4 52.5 all-gather.2
  161.0 53.2 reduce-scatter.2
  218.6 92.5 reduce-scatter.4
